TPU v7x, 128 devices: a whole 4x4x4 slice. The times are simulated.
128 devices in a mesh: grp: 4 (over z_hi, core), dom: 32 (over x, z_lo, y).
Axes of the slice: x: 4, y: 4, z: 4 (z_hi: 2, z_lo: 2; z = z_hi * 2 + z_lo), core: 2. Of those that a mesh axis runs over, the one named last changes fastest.
Arguments:
- emb: bfloat16 [32, 4096, 256], P('dom', 'grp'), may hold values from -4.5 to 4.5
- rel: float32 [256], replicated, may hold values from 0.5 to 2
- round_key: int32 [1], replicated, may hold values from 1 to 31
- edge_src: int32 [4, 32, 16, 128], P('grp', 'dom'), may hold values from 0 to 4095
- edge_dst: int32 [4, 32, 16, 128], P('grp', 'dom'), may hold values from 0 to 4095
- neg_idx: int32 [4, 32, 16, 128], P('grp', 'dom'), may hold values from 0 to 4095
- block_count: int32 [4, 32, 2], P('grp', 'dom'), may hold values from 1 to 8
Outputs:
- emb_grad: float32 [32, 4096, 256], P('dom', 'grp')
Inputs may be any that keep to these rules, and one draw needn't show every extreme that they name: Partition p is matched with partition p XOR round_key[0]; round_key is the same on every device. `edge_src`: row numbers within a partition. `edge_dst`: row numbers within a partition. `neg_idx`: row numbers within a partition.
All inputs are finite; a program needn't handle non-finite values.
Results may differ from a plain program's by a relative error of at most 0.009.
Values may be sent and summed in bfloat16 or wider, within the bound.
No kernel may reach another device: no remote copies, remote signals or barrier semaphores. Data moves between devices by JAX's collectives and lax.ppermute only.
A program may use at most 64 MiB of HBM per device.

v0:
```python
import jax
import jax.numpy as jnp
from jax import lax
from jax.sharding import PartitionSpec as P
from jax.experimental import pallas as pl


def swap_with_partner(payload, round_key, axis):
    count = lax.axis_size(axis)

    def branch(key):
        route = [(i, i ^ key) for i in range(count)]
        return lambda x: jax.tree.map(lambda a: lax.ppermute(a, axis, route), x)

    branches = [branch(key) for key in range(1, count)]
    return lax.switch(round_key - 1, branches, payload)


def one_hot(index, rows):
    flat = index.reshape(-1)
    return (flat[:, None] == jnp.arange(rows, dtype=jnp.int32)[None, :]).astype(jnp.bfloat16)


def pick_rows(table, index):
    hot = one_hot(index, table.shape[0])
    return jnp.dot(hot, table, preferred_element_type=jnp.float32).astype(jnp.bfloat16)


def scatter_rows(where, grads, rows, tile_rows=512, tile_edges=6144):
    edges, depth = grads.shape

    def kernel(where_ref, grads_ref, out_ref):
        i = pl.program_id(0)

        @pl.when(pl.program_id(1) == 0)
        def _():
            out_ref[...] = jnp.zeros_like(out_ref)

        ids = i * tile_rows + lax.broadcasted_iota(jnp.int32, (tile_rows, tile_edges), 0)
        hot = (ids == where_ref[...]).astype(jnp.bfloat16)
        out_ref[...] += jnp.dot(hot, grads_ref[...], preferred_element_type=jnp.float32)

    return pl.pallas_call(
        kernel,
        grid=(rows // tile_rows, edges // tile_edges),
        in_specs=[
            pl.BlockSpec((1, tile_edges), lambda i, k: (0, k)),
            pl.BlockSpec((tile_edges, depth), lambda i, k: (k, 0)),
        ],
        out_specs=pl.BlockSpec((tile_rows, depth), lambda i, k: (i, 0)),
        out_shape=jax.ShapeDtypeStruct((rows, depth), jnp.float32),
        cost_estimate=pl.CostEstimate(
            flops=2 * rows * edges * depth,
            transcendentals=0,
            bytes_accessed=edges * depth * 2 + rows * depth * 4 + edges * 4,
        ),
    )(where.reshape(1, edges), grads)


def pack_indices(parts, width):
    flat = jnp.concatenate([p.reshape(-1) for p in parts])
    halves = jnp.stack([jnp.right_shift(flat, 6), jnp.bitwise_and(flat, 63)])
    return halves.astype(jnp.bfloat16).reshape(-1, width)


def unpack_indices(packed, count, shape):
    halves = packed.reshape(2, -1).astype(jnp.int32)
    flat = halves[0] * 64 + halves[1]
    return [flat[i * flat.shape[0] // count:(i + 1) * flat.shape[0] // count].reshape(shape)
            for i in range(count)]


def block_grads(query, dst_rows, neg_rows, rel, count):
    blocks, width, depth = query.shape
    scale = depth ** (-0.5)
    dst_rows = dst_rows.reshape(blocks, width, depth)
    neg_rows = neg_rows.reshape(blocks, width, depth)
    cand = jnp.concatenate([dst_rows, neg_rows], axis=1)
    logits = jnp.einsum("bed,bcd->bec", query, cand, preferred_element_type=jnp.float32)
    probs = jax.nn.softmax(logits, axis=-1)
    live = (jnp.arange(blocks, dtype=jnp.int32) < count).astype(jnp.float32)
    target = jnp.eye(width, 2 * width, dtype=jnp.float32)
    weights = ((probs - target) * live[:, None, None]).astype(jnp.bfloat16)
    grad_query = jnp.einsum("bec,bcd->bed", weights, cand, preferred_element_type=jnp.float32)
    src_grad = (grad_query * rel * scale).astype(jnp.bfloat16)
    cand_grad = jnp.einsum(
        "bec,bed->bcd", weights, query, preferred_element_type=jnp.float32
    ).astype(jnp.bfloat16)
    return src_grad, cand_grad[:, :width], cand_grad[:, width:]


def on_device(emb, rel, round_key, edge_src, edge_dst, neg_idx, block_count):
    owners = lax.axis_size("grp")
    shard = emb[0]
    copies = jnp.broadcast_to(shard[None], (owners,) + shard.shape)
    table = lax.all_to_all(copies, "grp", 0, 0, tiled=True).reshape(-1, shard.shape[-1])
    rows, depth = table.shape
    scale = depth ** (-0.5)
    sources = edge_src[0, 0]
    targets = edge_dst[0, 0]
    negatives = neg_idx[0, 0]
    counts = block_count[0, 0]
    blocks = sources.shape[0] // 2
    width = sources.shape[1]

    edges = blocks * width
    own_rows = pick_rows(
        table,
        jnp.concatenate(
            [sources.reshape(-1), targets[:blocks].reshape(-1), negatives[:blocks].reshape(-1)]
        ),
    )
    src_rows = own_rows[: 2 * edges]
    query = (
        (src_rows.astype(jnp.float32) * rel * scale)
        .astype(jnp.bfloat16)
        .reshape(2 * blocks, width, depth)
    )
    packed = pack_indices([targets[blocks:], negatives[blocks:]], depth)
    tail = jnp.zeros((32 - packed.shape[0], depth), jnp.bfloat16)
    tail = tail.at[0].set(counts[1].astype(jnp.bfloat16))
    sent = jnp.concatenate([query[blocks:].reshape(-1, depth), packed, tail])
    got = swap_with_partner(sent, round_key[0], "dom")
    got_query = got[: blocks * width].reshape(blocks, width, depth)
    got_pack = got[blocks * width : blocks * width + packed.shape[0]]
    got_dst, got_neg = unpack_indices(got_pack, 2, (blocks, width))
    got_count = got[blocks * width + packed.shape[0], 0:1].astype(jnp.int32)

    sg_a, dg_a, ng_a = block_grads(
        query[:blocks], own_rows[2 * edges : 3 * edges], own_rows[3 * edges :], rel, counts[0]
    )
    got_rows = pick_rows(table, jnp.concatenate([got_dst.reshape(-1), got_neg.reshape(-1)]))
    sg_m, dg_m, ng_m = block_grads(
        got_query, got_rows[:edges], got_rows[edges:], rel, got_count[0]
    )
    sg_b = swap_with_partner(sg_m, round_key[0], "dom")

    where = jnp.concatenate(
        [sources.reshape(-1), targets[:blocks].reshape(-1), negatives[:blocks].reshape(-1),
         got_dst.reshape(-1), got_neg.reshape(-1)]
    )
    grads = jnp.concatenate(
        [g.reshape(-1, depth) for g in (sg_a, sg_b, dg_a, ng_a, dg_m, ng_m)]
    )
    owners = lax.axis_size("grp")
    share = rows // owners
    me = lax.axis_index("grp")
    keep = (jnp.arange(owners, dtype=jnp.int32) == me)[:, None, None]
    part = scatter_rows(where, grads, rows).reshape(owners, share, depth)
    got_parts = lax.all_to_all(part.astype(jnp.bfloat16), "grp", 0, 0, tiled=True)
    own = lax.dynamic_index_in_dim(part, me, axis=0)
    return jnp.sum(jnp.where(keep, own, got_parts.astype(jnp.float32)), axis=0)[None]


def solution(mesh):
    return jax.shard_map(
        on_device,
        mesh=mesh,
        in_specs=(
            P("dom", "grp", None),
            P(),
            P(),
            P("grp", "dom", None, None),
            P("grp", "dom", None, None),
            P("grp", "dom", None, None),
            P("grp", "dom", None),
        ),
        out_specs=P("dom", "grp", None),
        check_vma=False,
    )
```

profile of v0, /device:TPU:1, one launch (start us, length us, event | category | flops | bytes accessed | tf_op | source)
XLA Modules:
  0.0 158.5 jit_solution(9783371115206022355)
XLA Ops:
  0.0 2.5 %broadcast_in_dim.20 = bf16[4,1024,256]{2,1,0:T(8,128)(2,1)} broadcast(bf16[1024,256]{1,0:T(8,128)(2,1)} %bitcast.81), dimensions={1,2} | broadcast | bytes 2621440 | tf_op jit(solution)/shard_map/broadcast_in_dim | solution.py:95
  2.5 6.8 %all-to-all-start = ((bf16[4,1024,256]{2,1,0:T(8,128)(2,1)}), bf16[4,1024,256]{2,1,0:T(8,128)(2,1)S(1)}, u32[]{:S(2)}, u32[]{:S(2)}) async-start(bf16[4,1024,256]{2,1,0:T(8,128)(2,1)} %broadcast_in_dim.20), calls=%async_computation | async-start | bytes 4194304 | tf_op jit(solution)/shard_map/all_to_all | solution.py:96
  11.4 24.1 %all-to-all-done = bf16[4,1024,256]{2,1,0:T(8,128)(2,1)S(1)} async-done(((bf16[4,1024,256]{2,1,0:T(8,128)(2,1)}), bf16[4,1024,256]{2,1,0:T(8,128)(2,1)S(1)}, u32[]{:S(2)}, u32[]{:S(2)}) %all-to-all-start) | async-done | bytes 2097184 | tf_op jit(solution)/shard_map/all_to_all | solution.py:96
  35.5 12.3 %fusion.8 = bf16[4096,256]{1,0:T(8,128)(2,1)S(1)} fusion(bf16[4096,256]{1,0:T(8,128)(2,1)S(1)} %bitcast.75, s32[4096]{0:T(1024)S(1)} %pad_add_fusion.1), kind=kOutput, calls=%fused_computation.10 | convolution fusion | flops 8607760384 | bytes 4210688 | tf_op jit(solution)/shard_map/dot_general | solution.py:26
  49.8 3.0 %fusion.24 = bf16[8,128,256]{2,1,0:T(8,128)(2,1)} fusion(bf16[8,128,256]{2,1,0:T(8,128)(2,1)} %bitcast.87, bf16[8,128,256]{2,1,0:T(8,128)(2,1)S(1)} %bitcast.85, f32[256]{0:T(256)S(1)} %copy-done.8, f32[8]{0:T(128)S(1)} %compare_convert_fusion.1, f32[128,256]{1,0:T(8,128)S(1)} %fusion.36, bf16[8,128,256]{2,1,0:T(8,128)(2,1)} %bitcast.89), kind=kOutput, calls=%fused_computation.32 | convolution fusion | flops 274729472 | bytes 2229280 | tf_op jit(solution)/shard_map/bec,bcd->bed/dot_general | solution.py:84
  52.8 3.6 %convolution_convert_fusion.1 = bf16[8,256,256]{2,1,0:T(8,128)(2,1)} fusion(bf16[8,128,256]{2,1,0:T(8,128)(2,1)} %bitcast.90, f32[8]{0:T(128)S(1)} %compare_convert_fusion.1, f32[128,256]{1,0:T(8,128)S(1)} %fusion.36, bf16[8,128,256]{2,1,0:T(8,128)(2,1)} %bitcast.88, bf16[8,128,256]{2,1,0:T(8,128)(2,1)S(1)} %bitcast.86), kind=kOutput, calls=%fused_computation.19 | convolution fusion | flops 272370176 | bytes 2752544 | tf_op jit(solution)/shard_map/bec,bed->bcd/dot_general | solution.py:86
  56.6 14.4 %conditional.2 = (bf16[1056,256]{1,0:T(8,128)(2,1)}) conditional(s32[]{:T(128)} %bitcast.34, bf16[1056,256]{1,0:T(8,128)(2,1)S(1)} %maximum_maximum_fusion, bf16[1056,256]{1,0:T(8,128)(2,1)S(1)} %maximum_maximum_fusion, bf16[1056,256]{1,0:T(8,128)(2,1)S(1)} %maximum_maximum_fusion, ...), branch_computations={%region_0.0_spmd, %region_1.0_spmd, %region_2.0_spmd, %region_3.0_... | conditional | bytes 2162736 | solution.py:16
  56.6 2.8 %collective-permute-start.2 = (bf16[1056,256]{1,0:T(8,128)(2,1)S(1)}, bf16[1056,256]{1,0:T(8,128)(2,1)}, u32[]{:S(2)}, u32[]{:S(2)}) collective-permute-start(bf16[1056,256]{1,0:T(8,128)(2,1)S(1)} %param.4), channel_id=1, source_target_pairs={{0,3},{1,2},{2,1},{3,0},{4,7},{5,6},{6,5},{7,4},{8,11},{9,10},{10,... | collective-permute-start | bytes 1622024 | tf_op jit(solution)/shard_map/cond/branch_2_fun/ppermute | solution.py:13
  59.4 11.6 %collective-permute-done.2 = bf16[1056,256]{1,0:T(8,128)(2,1)} collective-permute-done((bf16[1056,256]{1,0:T(8,128)(2,1)S(1)}, bf16[1056,256]{1,0:T(8,128)(2,1)}, u32[]{:S(2)}, u32[]{:S(2)}) %collective-permute-start.2) | collective-permute-done | bytes 540704 | tf_op jit(solution)/shard_map/cond/branch_2_fun/ppermute | solution.py:13
  71.0 1.2 slice.133
  72.9 1.9 %slice.130 = bf16[1024,256]{1,0:T(8,128)(2,1)} slice(bf16[1056,256]{1,0:T(8,128)(2,1)} %get-tuple-element.162), slice={[0:1024], [0:256]} | slice | bytes 1048576 | tf_op jit(solution)/shard_map/slice | solution.py:124
  74.8 6.2 %fusion.9 = bf16[2048,256]{1,0:T(8,128)(2,1)S(1)} fusion(bf16[4096,256]{1,0:T(8,128)(2,1)S(1)} %bitcast.76, s32[2048]{0:T(1024)S(1)} %bitcast.95), kind=kOutput, calls=%fused_computation.12 | convolution fusion | flops 4303880192 | bytes 3153920 | tf_op jit(solution)/shard_map/dot_general | solution.py:26
  83.2 1.6 %fusion.25 = bf16[8,128,256]{2,1,0:T(8,128)(2,1)} fusion(bf16[8,128,256]{2,1,0:T(8,128)(2,1)S(1)} %bitcast.93, bf16[8,128,256]{2,1,0:T(8,128)(2,1)S(1)} %bitcast.91, f32[8]{0:T(128)S(1)} %compare_convert_fusion, f32[256]{0:T(256)S(1)} %copy-done.8, f32[128,256]{1,0:T(8,128)S(1)} %fusion.36, bf16[8,128,256]{2,1,0:T(8,128)(2,1)S(1)} %bitcast.83), kind=kOutput, calls=%fused_computation.33 | convolution fusion | flops 274729472 | bytes 2229280 | tf_op jit(solution)/shard_map/bec,bcd->bed/dot_general | solution.py:84
  84.8 2.4 %convolution_convert_fusion = bf16[8,256,256]{2,1,0:T(8,128)(2,1)S(1)} fusion(bf16[8,128,256]{2,1,0:T(8,128)(2,1)S(1)} %bitcast.84, f32[8]{0:T(128)S(1)} %compare_convert_fusion, f32[128,256]{1,0:T(8,128)S(1)} %fusion.36, bf16[8,128,256]{2,1,0:T(8,128)(2,1)} %bitcast.94, bf16[8,128,256]{2,1,0:T(8,128)(2,1)S(1)} %bitcast.92), kind=kOutput, calls=%fused_computation.18 | convolution fusion | flops 272370176 | bytes 2752544 | tf_op jit(solution)/shard_map/bec,bed->bcd/dot_general | solution.py:86
  87.3 13.4 %conditional.3 = (bf16[1024,256]{1,0:T(8,128)(2,1)}) conditional(s32[]{:T(128)} %bitcast.34, bf16[8,128,256]{2,1,0:T(8,128)(2,1)} %fusion.25, bf16[8,128,256]{2,1,0:T(8,128)(2,1)} %fusion.25, bf16[8,128,256]{2,1,0:T(8,128)(2,1)} %fusion.25, bf16[8,128,256]{2,1,0:T(8,128)(2,1)} %fusion.25, ...), branch_computations={%region_35.0_spmd, %region_36.0_spmd, %region_37.0_spmd, %region_3... | conditional | bytes 2097200 | solution.py:16
  87.3 2.7 %collective-permute-start.33 = (bf16[8,128,256]{2,1,0:T(8,128)(2,1)}, bf16[8,128,256]{2,1,0:T(8,128)(2,1)}, u32[]{:S(2)}, u32[]{:S(2)}) collective-permute-start(bf16[8,128,256]{2,1,0:T(8,128)(2,1)} %param.35), channel_id=1, source_target_pairs={{0,3},{1,2},{2,1},{3,0},{4,7},{5,6},{6,5},{7,4},{8,11},{9,10},{10,... | collective-permute-start | bytes 1572872 | tf_op jit(solution)/shard_map/cond/branch_2_fun/ppermute | solution.py:13
  90.0 10.7 %collective-permute-done.33 = bf16[8,128,256]{2,1,0:T(8,128)(2,1)} collective-permute-done((bf16[8,128,256]{2,1,0:T(8,128)(2,1)}, bf16[8,128,256]{2,1,0:T(8,128)(2,1)}, u32[]{:S(2)}, u32[]{:S(2)}) %collective-permute-start.33) | collective-permute-done | bytes 524320 | tf_op jit(solution)/shard_map/cond/branch_2_fun/ppermute | solution.py:13
  102.1 1.6 %copy-done.4 = bf16[6144,256]{1,0:T(8,128)(2,1)} copy-done((bf16[6144,256]{1,0:T(8,128)(2,1)}, bf16[6144,256]{1,0:T(8,128)(2,1)S(1)}, u32[]{:S(2)}) %copy-start.4) | copy-done | bytes 3145752
  103.7 17.1 %shard_map.73 = f32[4096,256]{1,0:T(8,128)} custom-call(s32[1,6144]{1,0:T(1,128)} %bitcast.99, bf16[6144,256]{1,0:T(8,128)(2,1)} %copy-done.4), custom_call_target="tpu_custom_call" | custom-call | flops 12884901888 | bytes 7364608 | tf_op jit(solution)/shard_map/pallas_call | solution.py:43
  120.8 3.7 %convert_element_type.183 = bf16[4,1024,256]{2,1,0:T(8,128)(2,1)} convert(f32[4,1024,256]{2,1,0:T(8,128)} %bitcast.73) | non-fusion elementwise | flops 1048576 | bytes 6291456 | tf_op jit(solution)/shard_map/convert_element_type | solution.py:150
  124.6 6.2 %all-to-all-start.1 = ((bf16[4,1024,256]{2,1,0:T(8,128)(2,1)}), bf16[4,1024,256]{2,1,0:T(8,128)(2,1)S(1)}, u32[]{:S(2)}, u32[]{:S(2)}) async-start(bf16[4,1024,256]{2,1,0:T(8,128)(2,1)} %convert_element_type.183), calls=%async_computation.1 | async-start | bytes 4194304 | tf_op jit(solution)/shard_map/all_to_all | solution.py:150
  130.8 1.3 dynamic-slice_bitcast_fusion
  132.1 24.9 %all-to-all-done.1 = bf16[4,1024,256]{2,1,0:T(8,128)(2,1)S(1)} async-done(((bf16[4,1024,256]{2,1,0:T(8,128)(2,1)}), bf16[4,1024,256]{2,1,0:T(8,128)(2,1)S(1)}, u32[]{:S(2)}, u32[]{:S(2)}) %all-to-all-start.1) | async-done | bytes 2097184 | tf_op jit(solution)/shard_map/all_to_all | solution.py:150
  157.0 1.5 select_reduce_fusion
  (48 shorter events, 7.3 us)
Async XLA Ops:
  2.5 7.4 %copy-start.9 = (s32[1,1,2]{2,1,0:T(1,128)S(1)}, s32[1,1,2]{2,1,0:T(1,128)}, u32[]{:S(2)}) copy-start(s32[1,1,2]{2,1,0:T(1,128)} %param.77) | copy-start | bytes 28
  2.5 8.0 %copy-start.6 = (s32[1,1,16,128]{3,2,1,0:T(8,128)S(1)}, s32[1,1,16,128]{3,2,1,0:T(8,128)}, u32[]{:S(2)}) copy-start(s32[1,1,16,128]{3,2,1,0:T(8,128)} %param.76) | copy-start | bytes 24580
  2.5 8.0 %copy-start.7 = (s32[1,1,16,128]{3,2,1,0:T(8,128)S(1)}, s32[1,1,16,128]{3,2,1,0:T(8,128)}, u32[]{:S(2)}) copy-start(s32[1,1,16,128]{3,2,1,0:T(8,128)} %param.75) | copy-start | bytes 24580
  2.5 8.9 %copy-start.5 = (s32[1,1,16,128]{3,2,1,0:T(8,128)S(1)}, s32[1,1,16,128]{3,2,1,0:T(8,128)}, u32[]{:S(2)}) copy-start(s32[1,1,16,128]{3,2,1,0:T(8,128)} %param.74) | copy-start | bytes 24580
  2.5 33.0 %all-to-all-start = ((bf16[4,1024,256]{2,1,0:T(8,128)(2,1)}), bf16[4,1024,256]{2,1,0:T(8,128)(2,1)S(1)}, u32[]{:S(2)}, u32[]{:S(2)}) async-start(bf16[4,1024,256]{2,1,0:T(8,128)(2,1)} %broadcast_in_dim.20), calls=%async_computation | async-start | bytes 4194304 | tf_op jit(solution)/shard_map/all_to_all | solution.py:96
  47.8 0.9 copy-start.8
  56.6 14.4 %collective-permute-start.2 = (bf16[1056,256]{1,0:T(8,128)(2,1)S(1)}, bf16[1056,256]{1,0:T(8,128)(2,1)}, u32[]{:S(2)}, u32[]{:S(2)}) collective-permute-start(bf16[1056,256]{1,0:T(8,128)(2,1)S(1)} %param.4), channel_id=1, source_target_pairs={{0,3},{1,2},{2,1},{3,0},{4,7},{5,6},{6,5},{7,4},{8,11},{9,10},{10,... | collective-permute-start | bytes 1622024 | tf_op jit(solution)/shard_map/cond/branch_2_fun/ppermute | solution.py:13
  81.0 2.1 %copy-start.2 = (bf16[1024,256]{1,0:T(8,128)(2,1)S(1)}, bf16[1024,256]{1,0:T(8,128)(2,1)}, u32[]{:S(2)}) copy-start(bf16[1024,256]{1,0:T(8,128)(2,1)} %slice.130) | copy-start | bytes 1572868
  82.4 0.8 copy-start.3
  84.8 2.4 %copy-start = (bf16[8,256,256]{2,1,0:T(8,128)(2,1)S(1)}, bf16[8,256,256]{2,1,0:T(8,128)(2,1)}, u32[]{:S(2)}) copy-start(bf16[8,256,256]{2,1,0:T(8,128)(2,1)} %convolution_convert_fusion.1) | copy-start | bytes 3145732
  87.3 13.5 %copy-start.1 = (bf16[8,128,256]{2,1,0:T(8,128)(2,1)S(1)}, bf16[8,128,256]{2,1,0:T(8,128)(2,1)}, u32[]{:S(2)}) copy-start(bf16[8,128,256]{2,1,0:T(8,128)(2,1)} %fusion.24) | copy-start | bytes 1572868
  87.3 13.3 %collective-permute-start.33 = (bf16[8,128,256]{2,1,0:T(8,128)(2,1)}, bf16[8,128,256]{2,1,0:T(8,128)(2,1)}, u32[]{:S(2)}, u32[]{:S(2)}) collective-permute-start(bf16[8,128,256]{2,1,0:T(8,128)(2,1)} %param.35), channel_id=1, source_target_pairs={{0,3},{1,2},{2,1},{3,0},{4,7},{5,6},{6,5},{7,4},{8,11},{9,10},{10,... | collective-permute-start | bytes 1572872 | tf_op jit(solution)/shard_map/cond/branch_2_fun/ppermute | solution.py:13
  102.1 1.6 %copy-start.4 = (bf16[6144,256]{1,0:T(8,128)(2,1)}, bf16[6144,256]{1,0:T(8,128)(2,1)S(1)}, u32[]{:S(2)}) copy-start(bf16[6144,256]{1,0:T(8,128)(2,1)S(1)} %constant_dynamic-update-slice_fusion.grads_ref) | copy-start | bytes 9437188
  124.6 32.4 %all-to-all-start.1 = ((bf16[4,1024,256]{2,1,0:T(8,128)(2,1)}), bf16[4,1024,256]{2,1,0:T(8,128)(2,1)S(1)}, u32[]{:S(2)}, u32[]{:S(2)}) async-start(bf16[4,1024,256]{2,1,0:T(8,128)(2,1)} %convert_element_type.183), calls=%async_computation.1 | async-start | bytes 4194304 | tf_op jit(solution)/shard_map/all_to_all | solution.py:150
where the time goes:
time: 159 us; the launch traced here: 158 us
  waiting for transfers between devices  71.2 us (45%)
  matrix products  29 us (18%)
  starting transfers between devices  18.5 us (12%)
  Pallas kernels  17.1 us (11%)
  local copies, waits for them, and re-layouts  13.2 us (8%)
  other arithmetic  7.86 us (5%)
    all_to_all x1, waiting for transfers between devices, on_device(): lax.all_to_all(part.astype(jnp.bfloat16), 'grp', 0, 0, tiled=True)  24.9 us
    all_to_all x1, waiting for transfers between devices, on_device(): lax.all_to_all(copies, 'grp', 0, 0, tiled=True).reshape(-1, shard.shape[-1])  24.1 us
    ppermute x2, waiting for transfers between devices, branch(): return lambda x: jax.tree.map(lambda a: lax.ppermute(a, axis, route), x)  22.2 us
    dot_general x2, matrix products, pick_rows(): jnp.dot(hot, table, preferred_element_type=jnp.float32).astype(jnp.bfloat16)  18.5 us
    pallas_call x1, Pallas kernels, scatter_rows(): pl.pallas_call(kernel, grid=(rows // tile_rows, edges // tile_edges), in_...  17.1 us
    all_to_all x1, starting transfers between devices, on_device(): lax.all_to_all(copies, 'grp', 0, 0, tiled=True).reshape(-1, shard.shape[-1])  6.78 us
    all_to_all x1, starting transfers between devices, on_device(): lax.all_to_all(part.astype(jnp.bfloat16), 'grp', 0, 0, tiled=True)  6.18 us
    dot_general x2, matrix products, block_grads(): jnp.einsum('bec,bed->bcd', weights, query, preferred_element_type=jnp.flo...  5.94 us
  transfers between devices with their start and end apart: 4, of which 4 were waited for; matrix products, arithmetic and copies ran while one was open for 2% of the time, Pallas kernels for 0%

commit v1 on v0

--- a/solution.py
+++ b/solution.py
@@ -26,33 +26,37 @@
     return jnp.dot(hot, table, preferred_element_type=jnp.float32).astype(jnp.bfloat16)
 
 
-def scatter_rows(where, grads, rows, tile_rows=512, tile_edges=6144):
+def scatter_rows(where, grads, rows, tile_rows=512):
     edges, depth = grads.shape
 
-    def kernel(where_ref, grads_ref, out_ref):
-        i = pl.program_id(0)
-
-        @pl.when(pl.program_id(1) == 0)
-        def _():
-            out_ref[...] = jnp.zeros_like(out_ref)
-
-        ids = i * tile_rows + lax.broadcasted_iota(jnp.int32, (tile_rows, tile_edges), 0)
+    def kernel(where_ref, grads_ref, out_ref, low_ref):
+        ids = pl.program_id(0) * tile_rows + lax.broadcasted_iota(
+            jnp.int32, (tile_rows, edges), 0
+        )
         hot = (ids == where_ref[...]).astype(jnp.bfloat16)
-        out_ref[...] += jnp.dot(hot, grads_ref[...], preferred_element_type=jnp.float32)
+        total = jnp.dot(hot, grads_ref[...], preferred_element_type=jnp.float32)
+        out_ref[...] = total
+        low_ref[...] = total.astype(jnp.bfloat16)
 
     return pl.pallas_call(
         kernel,
-        grid=(rows // tile_rows, edges // tile_edges),
+        grid=(rows // tile_rows,),
         in_specs=[
-            pl.BlockSpec((1, tile_edges), lambda i, k: (0, k)),
-            pl.BlockSpec((tile_edges, depth), lambda i, k: (k, 0)),
+            pl.BlockSpec((1, edges), lambda i: (0, 0)),
+            pl.BlockSpec((edges, depth), lambda i: (0, 0)),
         ],
-        out_specs=pl.BlockSpec((tile_rows, depth), lambda i, k: (i, 0)),
-        out_shape=jax.ShapeDtypeStruct((rows, depth), jnp.float32),
+        out_specs=[
+            pl.BlockSpec((tile_rows, depth), lambda i: (i, 0)),
+            pl.BlockSpec((tile_rows, depth), lambda i: (i, 0)),
+        ],
+        out_shape=[
+            jax.ShapeDtypeStruct((rows, depth), jnp.float32),
+            jax.ShapeDtypeStruct((rows, depth), jnp.bfloat16),
+        ],
         cost_estimate=pl.CostEstimate(
             flops=2 * rows * edges * depth,
             transcendentals=0,
-            bytes_accessed=edges * depth * 2 + rows * depth * 4 + edges * 4,
+            bytes_accessed=edges * depth * 2 + rows * depth * 6 + edges * 4,
         ),
     )(where.reshape(1, edges), grads)
 
@@ -146,8 +150,9 @@
     share = rows // owners
     me = lax.axis_index("grp")
     keep = (jnp.arange(owners, dtype=jnp.int32) == me)[:, None, None]
-    part = scatter_rows(where, grads, rows).reshape(owners, share, depth)
-    got_parts = lax.all_to_all(part.astype(jnp.bfloat16), "grp", 0, 0, tiled=True)
+    part, low = scatter_rows(where, grads, rows)
+    part = part.reshape(owners, share, depth)
+    got_parts = lax.all_to_all(low.reshape(owners, share, depth), "grp", 0, 0, tiled=True)
     own = lax.dynamic_index_in_dim(part, me, axis=0)
     return jnp.sum(jnp.where(keep, own, got_parts.astype(jnp.float32)), axis=0)[None]
 

time: 159 us -> 155 us (0.975); the launches traced: 158 us -> 152 us
  other arithmetic: 7.86 us -> 4.11 us
  starting transfers between devices: 18.5 us -> 15.6 us
    convert_element_type x1 -> x0, other arithmetic: 3.74 us -> none  [on_device(): part.astype(jnp.bfloat16)]
    ppermute x2, starting transfers between devices: 5.5 us -> 2.58 us  [branch(): return lambda x: jax.tree.map(lambda a: lax.ppermute(a, axis, route), x)]
where the time goes in v1:
time: 155 us; the launch traced here: 152 us
  waiting for transfers between devices  71.5 us (46%)
  matrix products  29 us (19%)
  Pallas kernels  17.2 us (11%)
  starting transfers between devices  15.6 us (10%)
  local copies, waits for them, and re-layouts  13.2 us (9%)
  other arithmetic  4.11 us (3%)
    all_to_all x1, waiting for transfers between devices, on_device(): lax.all_to_all(low.reshape(owners, share, depth), 'grp', 0, 0, tiled=True)  24.9 us
    all_to_all x1, waiting for transfers between devices, on_device(): lax.all_to_all(copies, 'grp', 0, 0, tiled=True).reshape(-1, shard.shape[-1])  24.1 us
    ppermute x2, waiting for transfers between devices, branch(): return lambda x: jax.tree.map(lambda a: lax.ppermute(a, axis, route), x)  22.5 us
    dot_general x2, matrix products, pick_rows(): jnp.dot(hot, table, preferred_element_type=jnp.float32).astype(jnp.bfloat16)  18.5 us
    pallas_call x1, Pallas kernels, scatter_rows(): pl.pallas_call(kernel, grid=(rows // tile_rows,), in_specs=[pl.BlockSpec(...  17.2 us
    all_to_all x1, starting transfers between devices, on_device(): lax.all_to_all(copies, 'grp', 0, 0, tiled=True).reshape(-1, shard.shape[-1])  6.78 us
    all_to_all x1, starting transfers between devices, on_device(): lax.all_to_all(low.reshape(owners, share, depth), 'grp', 0, 0, tiled=True)  6.26 us
    dot_general x2, matrix products, block_grads(): jnp.einsum('bec,bed->bcd', weights, query, preferred_element_type=jnp.flo...  5.93 us
  transfers between devices with their start and end apart: 4, of which 4 were waited for; matrix products, arithmetic and copies ran while one was open for 2% of the time, Pallas kernels for 0%

profile of v1, /device:TPU:1, one launch (start us, length us, event | category | flops | bytes accessed | tf_op | source)
XLA Modules:
  0.0 152.2 jit_solution(15082674912677242173)
XLA Ops:
  0.0 2.5 %broadcast_in_dim.20 = bf16[4,1024,256]{2,1,0:T(8,128)(2,1)} broadcast(bf16[1024,256]{1,0:T(8,128)(2,1)} %bitcast.81), dimensions={1,2} | broadcast | bytes 2621440 | tf_op jit(solution)/shard_map/broadcast_in_dim | solution.py:99
  2.5 6.8 %all-to-all-start = ((bf16[4,1024,256]{2,1,0:T(8,128)(2,1)}), bf16[4,1024,256]{2,1,0:T(8,128)(2,1)S(1)}, u32[]{:S(2)}, u32[]{:S(2)}) async-start(bf16[4,1024,256]{2,1,0:T(8,128)(2,1)} %broadcast_in_dim.20), calls=%async_computation | async-start | bytes 4194304 | tf_op jit(solution)/shard_map/all_to_all | solution.py:100
  11.5 24.1 %all-to-all-done = bf16[4,1024,256]{2,1,0:T(8,128)(2,1)S(1)} async-done(((bf16[4,1024,256]{2,1,0:T(8,128)(2,1)}), bf16[4,1024,256]{2,1,0:T(8,128)(2,1)S(1)}, u32[]{:S(2)}, u32[]{:S(2)}) %all-to-all-start) | async-done | bytes 2097184 | tf_op jit(solution)/shard_map/all_to_all | solution.py:100
  35.5 12.3 %fusion.8 = bf16[4096,256]{1,0:T(8,128)(2,1)S(1)} fusion(bf16[4096,256]{1,0:T(8,128)(2,1)S(1)} %bitcast.74, s32[4096]{0:T(1024)S(1)} %pad_add_fusion.1), kind=kOutput, calls=%fused_computation.10 | convolution fusion | flops 8607760384 | bytes 4210688 | tf_op jit(solution)/shard_map/dot_general | solution.py:26
  49.8 3.0 %fusion.24 = bf16[8,128,256]{2,1,0:T(8,128)(2,1)} fusion(bf16[8,128,256]{2,1,0:T(8,128)(2,1)} %bitcast.87, bf16[8,128,256]{2,1,0:T(8,128)(2,1)S(1)} %bitcast.85, f32[256]{0:T(256)S(1)} %copy-done.8, f32[8]{0:T(128)S(1)} %compare_convert_fusion.1, f32[128,256]{1,0:T(8,128)S(1)} %fusion.36, bf16[8,128,256]{2,1,0:T(8,128)(2,1)} %bitcast.89), kind=kOutput, calls=%fused_computation.32 | convolution fusion | flops 274729472 | bytes 2229280 | tf_op jit(solution)/shard_map/bec,bcd->bed/dot_general | solution.py:88
  52.8 3.6 %convolution_convert_fusion.1 = bf16[8,256,256]{2,1,0:T(8,128)(2,1)} fusion(bf16[8,128,256]{2,1,0:T(8,128)(2,1)} %bitcast.90, f32[8]{0:T(128)S(1)} %compare_convert_fusion.1, f32[128,256]{1,0:T(8,128)S(1)} %fusion.36, bf16[8,128,256]{2,1,0:T(8,128)(2,1)} %bitcast.88, bf16[8,128,256]{2,1,0:T(8,128)(2,1)S(1)} %bitcast.86), kind=kOutput, calls=%fused_computation.19 | convolution fusion | flops 272370176 | bytes 2752544 | tf_op jit(solution)/shard_map/bec,bed->bcd/dot_general | solution.py:90
  56.6 13.1 %conditional.2 = (bf16[1056,256]{1,0:T(8,128)(2,1)}) conditional(s32[]{:T(128)} %bitcast.34, bf16[1056,256]{1,0:T(8,128)(2,1)S(1)} %maximum_maximum_fusion, bf16[1056,256]{1,0:T(8,128)(2,1)S(1)} %maximum_maximum_fusion, bf16[1056,256]{1,0:T(8,128)(2,1)S(1)} %maximum_maximum_fusion, ...), branch_computations={%region_0.0_spmd, %region_1.0_spmd, %region_2.0_spmd, %region_3.0_... | conditional | bytes 2162736 | solution.py:16
  56.6 1.3 collective-permute-start.7
  57.9 11.8 %collective-permute-done.7 = bf16[1056,256]{1,0:T(8,128)(2,1)} collective-permute-done((bf16[1056,256]{1,0:T(8,128)(2,1)S(1)}, bf16[1056,256]{1,0:T(8,128)(2,1)}, u32[]{:S(2)}, u32[]{:S(2)}) %collective-permute-start.7) | collective-permute-done | bytes 540704 | tf_op jit(solution)/shard_map/cond/branch_7_fun/ppermute | solution.py:13
  69.7 1.2 slice.133
  71.6 1.9 %slice.130 = bf16[1024,256]{1,0:T(8,128)(2,1)} slice(bf16[1056,256]{1,0:T(8,128)(2,1)} %get-tuple-element.166), slice={[0:1024], [0:256]} | slice | bytes 1048576 | tf_op jit(solution)/shard_map/slice | solution.py:128
  73.5 6.2 %fusion.9 = bf16[2048,256]{1,0:T(8,128)(2,1)S(1)} fusion(bf16[4096,256]{1,0:T(8,128)(2,1)S(1)} %bitcast.75, s32[2048]{0:T(1024)S(1)} %bitcast.96), kind=kOutput, calls=%fused_computation.12 | convolution fusion | flops 4303880192 | bytes 3153920 | tf_op jit(solution)/shard_map/dot_general | solution.py:26
  81.8 1.7 %fusion.25 = bf16[8,128,256]{2,1,0:T(8,128)(2,1)} fusion(bf16[8,128,256]{2,1,0:T(8,128)(2,1)S(1)} %bitcast.93, bf16[8,128,256]{2,1,0:T(8,128)(2,1)S(1)} %bitcast.91, f32[8]{0:T(128)S(1)} %compare_convert_fusion, f32[256]{0:T(256)S(1)} %copy-done.8, f32[128,256]{1,0:T(8,128)S(1)} %fusion.36, bf16[8,128,256]{2,1,0:T(8,128)(2,1)S(1)} %bitcast.83), kind=kOutput, calls=%fused_computation.33 | convolution fusion | flops 274729472 | bytes 2229280 | tf_op jit(solution)/shard_map/bec,bcd->bed/dot_general | solution.py:88
  83.5 2.4 %convolution_convert_fusion = bf16[8,256,256]{2,1,0:T(8,128)(2,1)S(1)} fusion(bf16[8,128,256]{2,1,0:T(8,128)(2,1)S(1)} %bitcast.84, f32[8]{0:T(128)S(1)} %compare_convert_fusion, f32[128,256]{1,0:T(8,128)S(1)} %fusion.36, bf16[8,128,256]{2,1,0:T(8,128)(2,1)} %bitcast.94, bf16[8,128,256]{2,1,0:T(8,128)(2,1)S(1)} %bitcast.92), kind=kOutput, calls=%fused_computation.18 | convolution fusion | flops 272370176 | bytes 2752544 | tf_op jit(solution)/shard_map/bec,bed->bcd/dot_general | solution.py:90
  85.9 12.1 %conditional.3 = (bf16[1024,256]{1,0:T(8,128)(2,1)}) conditional(s32[]{:T(128)} %bitcast.34, bf16[8,128,256]{2,1,0:T(8,128)(2,1)} %fusion.25, bf16[8,128,256]{2,1,0:T(8,128)(2,1)} %fusion.25, bf16[8,128,256]{2,1,0:T(8,128)(2,1)} %fusion.25, bf16[8,128,256]{2,1,0:T(8,128)(2,1)} %fusion.25, ...), branch_computations={%region_35.0_spmd, %region_36.0_spmd, %region_37.0_spmd, %region_3... | conditional | bytes 2097200 | solution.py:16
  86.0 1.3 collective-permute-start.38
  87.2 10.8 %collective-permute-done.38 = bf16[8,128,256]{2,1,0:T(8,128)(2,1)} collective-permute-done((bf16[8,128,256]{2,1,0:T(8,128)(2,1)}, bf16[8,128,256]{2,1,0:T(8,128)(2,1)}, u32[]{:S(2)}, u32[]{:S(2)}) %collective-permute-start.38) | collective-permute-done | bytes 524320 | tf_op jit(solution)/shard_map/cond/branch_7_fun/ppermute | solution.py:13
  98.2 1.1 constant_dynamic-update-slice_fusion.4
  99.4 1.6 %copy-done.4 = bf16[6144,256]{1,0:T(8,128)(2,1)} copy-done((bf16[6144,256]{1,0:T(8,128)(2,1)}, bf16[6144,256]{1,0:T(8,128)(2,1)S(1)}, u32[]{:S(2)}) %copy-start.4) | copy-done | bytes 3145752
  101.1 17.2 %shard_map.73 = (f32[4096,256]{1,0:T(8,128)}, bf16[4096,256]{1,0:T(8,128)(2,1)}) custom-call(s32[1,6144]{1,0:T(1,128)} %bitcast.100, bf16[6144,256]{1,0:T(8,128)(2,1)} %copy-done.4), custom_call_target="tpu_custom_call" | custom-call | flops 12884901888 | bytes 9461760 | tf_op jit(solution)/shard_map/pallas_call | solution.py:41
  118.3 6.3 %all-to-all-start.1 = ((bf16[4,1024,256]{2,1,0:T(8,128)(2,1)}), bf16[4,1024,256]{2,1,0:T(8,128)(2,1)S(1)}, u32[]{:S(2)}, u32[]{:S(2)}) async-start(bf16[4,1024,256]{2,1,0:T(8,128)(2,1)} %bitcast.76), calls=%async_computation.1 | async-start | bytes 4194304 | tf_op jit(solution)/shard_map/all_to_all | solution.py:155
  124.6 1.3 dynamic-slice_bitcast_fusion
  125.8 24.9 %all-to-all-done.1 = bf16[4,1024,256]{2,1,0:T(8,128)(2,1)S(1)} async-done(((bf16[4,1024,256]{2,1,0:T(8,128)(2,1)}), bf16[4,1024,256]{2,1,0:T(8,128)(2,1)S(1)}, u32[]{:S(2)}, u32[]{:S(2)}) %all-to-all-start.1) | async-done | bytes 2097184 | tf_op jit(solution)/shard_map/all_to_all | solution.py:155
  150.8 1.5 select_reduce_fusion
  (47 shorter events, 6.2 us)
Async XLA Ops:
  2.5 7.4 %copy-start.9 = (s32[1,1,2]{2,1,0:T(1,128)S(1)}, s32[1,1,2]{2,1,0:T(1,128)}, u32[]{:S(2)}) copy-start(s32[1,1,2]{2,1,0:T(1,128)} %param.77) | copy-start | bytes 28
  2.5 8.0 %copy-start.6 = (s32[1,1,16,128]{3,2,1,0:T(8,128)S(1)}, s32[1,1,16,128]{3,2,1,0:T(8,128)}, u32[]{:S(2)}) copy-start(s32[1,1,16,128]{3,2,1,0:T(8,128)} %param.76) | copy-start | bytes 24580
  2.5 8.0 %copy-start.7 = (s32[1,1,16,128]{3,2,1,0:T(8,128)S(1)}, s32[1,1,16,128]{3,2,1,0:T(8,128)}, u32[]{:S(2)}) copy-start(s32[1,1,16,128]{3,2,1,0:T(8,128)} %param.75) | copy-start | bytes 24580
  2.5 8.9 %copy-start.5 = (s32[1,1,16,128]{3,2,1,0:T(8,128)S(1)}, s32[1,1,16,128]{3,2,1,0:T(8,128)}, u32[]{:S(2)}) copy-start(s32[1,1,16,128]{3,2,1,0:T(8,128)} %param.74) | copy-start | bytes 24580
  2.5 33.0 %all-to-all-start = ((bf16[4,1024,256]{2,1,0:T(8,128)(2,1)}), bf16[4,1024,256]{2,1,0:T(8,128)(2,1)S(1)}, u32[]{:S(2)}, u32[]{:S(2)}) async-start(bf16[4,1024,256]{2,1,0:T(8,128)(2,1)} %broadcast_in_dim.20), calls=%async_computation | async-start | bytes 4194304 | tf_op jit(solution)/shard_map/all_to_all | solution.py:100
  47.8 0.9 copy-start.8
  56.6 13.0 %collective-permute-start.7 = (bf16[1056,256]{1,0:T(8,128)(2,1)S(1)}, bf16[1056,256]{1,0:T(8,128)(2,1)}, u32[]{:S(2)}, u32[]{:S(2)}) collective-permute-start(bf16[1056,256]{1,0:T(8,128)(2,1)S(1)} %param.9), channel_id=1, source_target_pairs={{0,8},{1,9},{2,10},{3,11},{4,12},{5,13},{6,14},{7,15},{8,0},{9,1},... | collective-permute-start | bytes 1622024 | tf_op jit(solution)/shard_map/cond/branch_7_fun/ppermute | solution.py:13
  79.7 2.1 %copy-start.2 = (bf16[1024,256]{1,0:T(8,128)(2,1)S(1)}, bf16[1024,256]{1,0:T(8,128)(2,1)}, u32[]{:S(2)}) copy-start(bf16[1024,256]{1,0:T(8,128)(2,1)} %slice.130) | copy-start | bytes 1572868
  81.0 0.8 copy-start.3
  83.5 2.4 %copy-start = (bf16[8,256,256]{2,1,0:T(8,128)(2,1)S(1)}, bf16[8,256,256]{2,1,0:T(8,128)(2,1)}, u32[]{:S(2)}) copy-start(bf16[8,256,256]{2,1,0:T(8,128)(2,1)} %convolution_convert_fusion.1) | copy-start | bytes 3145732
  85.9 12.2 %copy-start.1 = (bf16[8,128,256]{2,1,0:T(8,128)(2,1)S(1)}, bf16[8,128,256]{2,1,0:T(8,128)(2,1)}, u32[]{:S(2)}) copy-start(bf16[8,128,256]{2,1,0:T(8,128)(2,1)} %fusion.24) | copy-start | bytes 1572868
  86.0 12.0 %collective-permute-start.38 = (bf16[8,128,256]{2,1,0:T(8,128)(2,1)}, bf16[8,128,256]{2,1,0:T(8,128)(2,1)}, u32[]{:S(2)}, u32[]{:S(2)}) collective-permute-start(bf16[8,128,256]{2,1,0:T(8,128)(2,1)} %param.40), channel_id=1, source_target_pairs={{0,8},{1,9},{2,10},{3,11},{4,12},{5,13},{6,14},{7,15},{8,0},{9,1},... | collective-permute-start | bytes 1572872 | tf_op jit(solution)/shard_map/cond/branch_7_fun/ppermute | solution.py:13
  99.4 1.7 %copy-start.4 = (bf16[6144,256]{1,0:T(8,128)(2,1)}, bf16[6144,256]{1,0:T(8,128)(2,1)S(1)}, u32[]{:S(2)}) copy-start(bf16[6144,256]{1,0:T(8,128)(2,1)S(1)} %constant_dynamic-update-slice_fusion.grads_ref) | copy-start | bytes 9437188
  118.3 32.5 %all-to-all-start.1 = ((bf16[4,1024,256]{2,1,0:T(8,128)(2,1)}), bf16[4,1024,256]{2,1,0:T(8,128)(2,1)S(1)}, u32[]{:S(2)}, u32[]{:S(2)}) async-start(bf16[4,1024,256]{2,1,0:T(8,128)(2,1)} %bitcast.76), calls=%async_computation.1 | async-start | bytes 4194304 | tf_op jit(solution)/shard_map/all_to_all | solution.py:155

commit v2 on v1

--- a/solution.py
+++ b/solution.py
@@ -26,7 +26,7 @@
     return jnp.dot(hot, table, preferred_element_type=jnp.float32).astype(jnp.bfloat16)
 
 
-def scatter_rows(where, grads, rows, tile_rows=512):
+def scatter_rows(where, grads, rows, tile_rows=256):
     edges, depth = grads.shape
 
     def kernel(where_ref, grads_ref, out_ref, low_ref):

time: 155 us -> 162 us (1.045); the launches traced: 152 us -> 162 us
  starting transfers between devices: 15.6 us -> 24 us
    ppermute x2, starting transfers between devices: 2.58 us -> 10.9 us  [branch(): return lambda x: jax.tree.map(lambda a: lax.ppermute(a, axis, route), x)]
where the time goes in v2:
time: 162 us
  waiting for transfers between devices  71.6 us (44%)
  matrix products  29 us (18%)
  starting transfers between devices  24 us (15%)
  Pallas kernels  18.6 us (11%)
  local copies, waits for them, and re-layouts  13.2 us (8%)
  other arithmetic  4.11 us (3%)
    all_to_all x1, waiting for transfers between devices, on_device(): lax.all_to_all(low.reshape(owners, share, depth), 'grp', 0, 0, tiled=True)  24.9 us
    all_to_all x1, waiting for transfers between devices, on_device(): lax.all_to_all(copies, 'grp', 0, 0, tiled=True).reshape(-1, shard.shape[-1])  24.1 us
    ppermute x2, waiting for transfers between devices, branch(): return lambda x: jax.tree.map(lambda a: lax.ppermute(a, axis, route), x)  22.6 us
    pallas_call x1, Pallas kernels, scatter_rows(): pl.pallas_call(kernel, grid=(rows // tile_rows,), in_specs=[pl.BlockSpec(...  18.6 us
    dot_general x2, matrix products, pick_rows(): jnp.dot(hot, table, preferred_element_type=jnp.float32).astype(jnp.bfloat16)  18.5 us
    ppermute x2, starting transfers between devices, branch(): return lambda x: jax.tree.map(lambda a: lax.ppermute(a, axis, route), x)  10.9 us
    all_to_all x1, starting transfers between devices, on_device(): lax.all_to_all(copies, 'grp', 0, 0, tiled=True).reshape(-1, shard.shape[-1])  6.78 us
    all_to_all x1, starting transfers between devices, on_device(): lax.all_to_all(low.reshape(owners, share, depth), 'grp', 0, 0, tiled=True)  6.25 us
  transfers between devices with their start and end apart: 4, of which 4 were waited for; matrix products, arithmetic and copies ran while one was open for 2% of the time, Pallas kernels for 0%

profile of v2, /device:TPU:1, one launch (start us, length us, event | category | flops | bytes accessed | tf_op | source)
XLA Modules:
  0.0 162.3 jit_solution(13937673164796741229)
XLA Ops:
  0.0 2.5 %broadcast_in_dim.20 = bf16[4,1024,256]{2,1,0:T(8,128)(2,1)} broadcast(bf16[1024,256]{1,0:T(8,128)(2,1)} %bitcast.81), dimensions={1,2} | broadcast | bytes 2621440 | tf_op jit(solution)/shard_map/broadcast_in_dim | solution.py:99
  2.5 6.8 %all-to-all-start = ((bf16[4,1024,256]{2,1,0:T(8,128)(2,1)}), bf16[4,1024,256]{2,1,0:T(8,128)(2,1)S(1)}, u32[]{:S(2)}, u32[]{:S(2)}) async-start(bf16[4,1024,256]{2,1,0:T(8,128)(2,1)} %broadcast_in_dim.20), calls=%async_computation | async-start | bytes 4194304 | tf_op jit(solution)/shard_map/all_to_all | solution.py:100
  11.5 24.1 %all-to-all-done = bf16[4,1024,256]{2,1,0:T(8,128)(2,1)S(1)} async-done(((bf16[4,1024,256]{2,1,0:T(8,128)(2,1)}), bf16[4,1024,256]{2,1,0:T(8,128)(2,1)S(1)}, u32[]{:S(2)}, u32[]{:S(2)}) %all-to-all-start) | async-done | bytes 2097184 | tf_op jit(solution)/shard_map/all_to_all | solution.py:100
  35.5 12.3 %fusion.8 = bf16[4096,256]{1,0:T(8,128)(2,1)S(1)} fusion(bf16[4096,256]{1,0:T(8,128)(2,1)S(1)} %bitcast.74, s32[4096]{0:T(1024)S(1)} %pad_add_fusion.1), kind=kOutput, calls=%fused_computation.10 | convolution fusion | flops 8607760384 | bytes 4210688 | tf_op jit(solution)/shard_map/dot_general | solution.py:26
  49.8 3.0 %fusion.24 = bf16[8,128,256]{2,1,0:T(8,128)(2,1)} fusion(bf16[8,128,256]{2,1,0:T(8,128)(2,1)} %bitcast.87, bf16[8,128,256]{2,1,0:T(8,128)(2,1)S(1)} %bitcast.85, f32[256]{0:T(256)S(1)} %copy-done.8, f32[8]{0:T(128)S(1)} %compare_convert_fusion.1, f32[128,256]{1,0:T(8,128)S(1)} %fusion.36, bf16[8,128,256]{2,1,0:T(8,128)(2,1)} %bitcast.89), kind=kOutput, calls=%fused_computation.32 | convolution fusion | flops 274729472 | bytes 2229280 | tf_op jit(solution)/shard_map/bec,bcd->bed/dot_general | solution.py:88
  52.8 3.6 %convolution_convert_fusion.1 = bf16[8,256,256]{2,1,0:T(8,128)(2,1)} fusion(bf16[8,128,256]{2,1,0:T(8,128)(2,1)} %bitcast.90, f32[8]{0:T(128)S(1)} %compare_convert_fusion.1, f32[128,256]{1,0:T(8,128)S(1)} %fusion.36, bf16[8,128,256]{2,1,0:T(8,128)(2,1)} %bitcast.88, bf16[8,128,256]{2,1,0:T(8,128)(2,1)S(1)} %bitcast.86), kind=kOutput, calls=%fused_computation.19 | convolution fusion | flops 272370176 | bytes 2752544 | tf_op jit(solution)/shard_map/bec,bed->bcd/dot_general | solution.py:90
  56.6 17.3 %conditional.2 = (bf16[1056,256]{1,0:T(8,128)(2,1)}) conditional(s32[]{:T(128)} %bitcast.34, bf16[1056,256]{1,0:T(8,128)(2,1)S(1)} %maximum_maximum_fusion, bf16[1056,256]{1,0:T(8,128)(2,1)S(1)} %maximum_maximum_fusion, bf16[1056,256]{1,0:T(8,128)(2,1)S(1)} %maximum_maximum_fusion, ...), branch_computations={%region_0.0_spmd, %region_1.0_spmd, %region_2.0_spmd, %region_3.0_... | conditional | bytes 2162736 | solution.py:16
  56.6 5.5 %collective-permute-start.30 = (bf16[1056,256]{1,0:T(8,128)(2,1)S(1)}, bf16[1056,256]{1,0:T(8,128)(2,1)}, u32[]{:S(2)}, u32[]{:S(2)}) collective-permute-start(bf16[1056,256]{1,0:T(8,128)(2,1)S(1)} %param.32), channel_id=1, source_target_pairs={{0,31},{1,30},{2,29},{3,28},{4,27},{5,26},{6,25},{7,24},{8,23},{9,... | collective-permute-start | bytes 1622024 | tf_op jit(solution)/shard_map/cond/branch_30_fun/ppermute | solution.py:13
  62.1 11.8 %collective-permute-done.30 = bf16[1056,256]{1,0:T(8,128)(2,1)} collective-permute-done((bf16[1056,256]{1,0:T(8,128)(2,1)S(1)}, bf16[1056,256]{1,0:T(8,128)(2,1)}, u32[]{:S(2)}, u32[]{:S(2)}) %collective-permute-start.30) | collective-permute-done | bytes 540704 | tf_op jit(solution)/shard_map/cond/branch_30_fun/ppermute | solution.py:13
  73.9 1.2 slice.133
  75.8 1.9 %slice.130 = bf16[1024,256]{1,0:T(8,128)(2,1)} slice(bf16[1056,256]{1,0:T(8,128)(2,1)} %get-tuple-element.166), slice={[0:1024], [0:256]} | slice | bytes 1048576 | tf_op jit(solution)/shard_map/slice | solution.py:128
  77.7 6.2 %fusion.9 = bf16[2048,256]{1,0:T(8,128)(2,1)S(1)} fusion(bf16[4096,256]{1,0:T(8,128)(2,1)S(1)} %bitcast.75, s32[2048]{0:T(1024)S(1)} %bitcast.96), kind=kOutput, calls=%fused_computation.12 | convolution fusion | flops 4303880192 | bytes 3153920 | tf_op jit(solution)/shard_map/dot_general | solution.py:26
  86.0 1.6 %fusion.25 = bf16[8,128,256]{2,1,0:T(8,128)(2,1)} fusion(bf16[8,128,256]{2,1,0:T(8,128)(2,1)S(1)} %bitcast.93, bf16[8,128,256]{2,1,0:T(8,128)(2,1)S(1)} %bitcast.91, f32[8]{0:T(128)S(1)} %compare_convert_fusion, f32[256]{0:T(256)S(1)} %copy-done.8, f32[128,256]{1,0:T(8,128)S(1)} %fusion.36, bf16[8,128,256]{2,1,0:T(8,128)(2,1)S(1)} %bitcast.83), kind=kOutput, calls=%fused_computation.33 | convolution fusion | flops 274729472 | bytes 2229280 | tf_op jit(solution)/shard_map/bec,bcd->bed/dot_general | solution.py:88
  87.7 2.4 %convolution_convert_fusion = bf16[8,256,256]{2,1,0:T(8,128)(2,1)S(1)} fusion(bf16[8,128,256]{2,1,0:T(8,128)(2,1)S(1)} %bitcast.84, f32[8]{0:T(128)S(1)} %compare_convert_fusion, f32[128,256]{1,0:T(8,128)S(1)} %fusion.36, bf16[8,128,256]{2,1,0:T(8,128)(2,1)} %bitcast.94, bf16[8,128,256]{2,1,0:T(8,128)(2,1)S(1)} %bitcast.92), kind=kOutput, calls=%fused_computation.18 | convolution fusion | flops 272370176 | bytes 2752544 | tf_op jit(solution)/shard_map/bec,bed->bcd/dot_general | solution.py:90
  90.2 16.5 %conditional.3 = (bf16[1024,256]{1,0:T(8,128)(2,1)}) conditional(s32[]{:T(128)} %bitcast.34, bf16[8,128,256]{2,1,0:T(8,128)(2,1)} %fusion.25, bf16[8,128,256]{2,1,0:T(8,128)(2,1)} %fusion.25, bf16[8,128,256]{2,1,0:T(8,128)(2,1)} %fusion.25, bf16[8,128,256]{2,1,0:T(8,128)(2,1)} %fusion.25, ...), branch_computations={%region_35.0_spmd, %region_36.0_spmd, %region_37.0_spmd, %region_3... | conditional | bytes 2097200 | solution.py:16
  90.4 5.5 %collective-permute-start.61 = (bf16[8,128,256]{2,1,0:T(8,128)(2,1)}, bf16[8,128,256]{2,1,0:T(8,128)(2,1)}, u32[]{:S(2)}, u32[]{:S(2)}) collective-permute-start(bf16[8,128,256]{2,1,0:T(8,128)(2,1)} %param.63), channel_id=1, source_target_pairs={{0,31},{1,30},{2,29},{3,28},{4,27},{5,26},{6,25},{7,24},{8,23},{9,... | collective-permute-start | bytes 1572872 | tf_op jit(solution)/shard_map/cond/branch_30_fun/ppermute | solution.py:13
  95.9 10.8 %collective-permute-done.61 = bf16[8,128,256]{2,1,0:T(8,128)(2,1)} collective-permute-done((bf16[8,128,256]{2,1,0:T(8,128)(2,1)}, bf16[8,128,256]{2,1,0:T(8,128)(2,1)}, u32[]{:S(2)}, u32[]{:S(2)}) %collective-permute-start.61) | collective-permute-done | bytes 524320 | tf_op jit(solution)/shard_map/cond/branch_30_fun/ppermute | solution.py:13
  106.9 1.1 constant_dynamic-update-slice_fusion.4
  108.1 1.6 %copy-done.4 = bf16[6144,256]{1,0:T(8,128)(2,1)} copy-done((bf16[6144,256]{1,0:T(8,128)(2,1)}, bf16[6144,256]{1,0:T(8,128)(2,1)S(1)}, u32[]{:S(2)}) %copy-start.4) | copy-done | bytes 3145752
  109.8 18.6 %shard_map.73 = (f32[4096,256]{1,0:T(8,128)}, bf16[4096,256]{1,0:T(8,128)(2,1)}) custom-call(s32[1,6144]{1,0:T(1,128)} %bitcast.100, bf16[6144,256]{1,0:T(8,128)(2,1)} %copy-done.4), custom_call_target="tpu_custom_call" | custom-call | flops 12884901888 | bytes 9461760 | tf_op jit(solution)/shard_map/pallas_call | solution.py:41
  128.3 6.3 %all-to-all-start.1 = ((bf16[4,1024,256]{2,1,0:T(8,128)(2,1)}), bf16[4,1024,256]{2,1,0:T(8,128)(2,1)S(1)}, u32[]{:S(2)}, u32[]{:S(2)}) async-start(bf16[4,1024,256]{2,1,0:T(8,128)(2,1)} %bitcast.76), calls=%async_computation.1 | async-start | bytes 4194304 | tf_op jit(solution)/shard_map/all_to_all | solution.py:155
  134.6 1.3 dynamic-slice_bitcast_fusion
  135.9 24.9 %all-to-all-done.1 = bf16[4,1024,256]{2,1,0:T(8,128)(2,1)S(1)} async-done(((bf16[4,1024,256]{2,1,0:T(8,128)(2,1)}), bf16[4,1024,256]{2,1,0:T(8,128)(2,1)S(1)}, u32[]{:S(2)}, u32[]{:S(2)}) %all-to-all-start.1) | async-done | bytes 2097184 | tf_op jit(solution)/shard_map/all_to_all | solution.py:155
  160.8 1.5 select_reduce_fusion
  (47 shorter events, 6.2 us)
Async XLA Ops:
  2.5 7.4 %copy-start.9 = (s32[1,1,2]{2,1,0:T(1,128)S(1)}, s32[1,1,2]{2,1,0:T(1,128)}, u32[]{:S(2)}) copy-start(s32[1,1,2]{2,1,0:T(1,128)} %param.77) | copy-start | bytes 28
  2.5 8.0 %copy-start.6 = (s32[1,1,16,128]{3,2,1,0:T(8,128)S(1)}, s32[1,1,16,128]{3,2,1,0:T(8,128)}, u32[]{:S(2)}) copy-start(s32[1,1,16,128]{3,2,1,0:T(8,128)} %param.76) | copy-start | bytes 24580
  2.5 8.0 %copy-start.7 = (s32[1,1,16,128]{3,2,1,0:T(8,128)S(1)}, s32[1,1,16,128]{3,2,1,0:T(8,128)}, u32[]{:S(2)}) copy-start(s32[1,1,16,128]{3,2,1,0:T(8,128)} %param.75) | copy-start | bytes 24580
  2.5 8.9 %copy-start.5 = (s32[1,1,16,128]{3,2,1,0:T(8,128)S(1)}, s32[1,1,16,128]{3,2,1,0:T(8,128)}, u32[]{:S(2)}) copy-start(s32[1,1,16,128]{3,2,1,0:T(8,128)} %param.74) | copy-start | bytes 24580
  2.5 33.0 %all-to-all-start = ((bf16[4,1024,256]{2,1,0:T(8,128)(2,1)}), bf16[4,1024,256]{2,1,0:T(8,128)(2,1)S(1)}, u32[]{:S(2)}, u32[]{:S(2)}) async-start(bf16[4,1024,256]{2,1,0:T(8,128)(2,1)} %broadcast_in_dim.20), calls=%async_computation | async-start | bytes 4194304 | tf_op jit(solution)/shard_map/all_to_all | solution.py:100
  47.8 0.9 copy-start.8
  56.6 17.3 %collective-permute-start.30 = (bf16[1056,256]{1,0:T(8,128)(2,1)S(1)}, bf16[1056,256]{1,0:T(8,128)(2,1)}, u32[]{:S(2)}, u32[]{:S(2)}) collective-permute-start(bf16[1056,256]{1,0:T(8,128)(2,1)S(1)} %param.32), channel_id=1, source_target_pairs={{0,31},{1,30},{2,29},{3,28},{4,27},{5,26},{6,25},{7,24},{8,23},{9,... | collective-permute-start | bytes 1622024 | tf_op jit(solution)/shard_map/cond/branch_30_fun/ppermute | solution.py:13
  83.9 2.1 %copy-start.2 = (bf16[1024,256]{1,0:T(8,128)(2,1)S(1)}, bf16[1024,256]{1,0:T(8,128)(2,1)}, u32[]{:S(2)}) copy-start(bf16[1024,256]{1,0:T(8,128)(2,1)} %slice.130) | copy-start | bytes 1572868
  85.2 0.8 copy-start.3
  87.7 2.4 %copy-start = (bf16[8,256,256]{2,1,0:T(8,128)(2,1)S(1)}, bf16[8,256,256]{2,1,0:T(8,128)(2,1)}, u32[]{:S(2)}) copy-start(bf16[8,256,256]{2,1,0:T(8,128)(2,1)} %convolution_convert_fusion.1) | copy-start | bytes 3145732
  90.2 16.6 %copy-start.1 = (bf16[8,128,256]{2,1,0:T(8,128)(2,1)S(1)}, bf16[8,128,256]{2,1,0:T(8,128)(2,1)}, u32[]{:S(2)}) copy-start(bf16[8,128,256]{2,1,0:T(8,128)(2,1)} %fusion.24) | copy-start | bytes 1572868
  90.4 16.3 %collective-permute-start.61 = (bf16[8,128,256]{2,1,0:T(8,128)(2,1)}, bf16[8,128,256]{2,1,0:T(8,128)(2,1)}, u32[]{:S(2)}, u32[]{:S(2)}) collective-permute-start(bf16[8,128,256]{2,1,0:T(8,128)(2,1)} %param.63), channel_id=1, source_target_pairs={{0,31},{1,30},{2,29},{3,28},{4,27},{5,26},{6,25},{7,24},{8,23},{9,... | collective-permute-start | bytes 1572872 | tf_op jit(solution)/shard_map/cond/branch_30_fun/ppermute | solution.py:13
  108.1 1.7 %copy-start.4 = (bf16[6144,256]{1,0:T(8,128)(2,1)}, bf16[6144,256]{1,0:T(8,128)(2,1)S(1)}, u32[]{:S(2)}) copy-start(bf16[6144,256]{1,0:T(8,128)(2,1)S(1)} %constant_dynamic-update-slice_fusion.grads_ref) | copy-start | bytes 9437188
  128.3 32.5 %all-to-all-start.1 = ((bf16[4,1024,256]{2,1,0:T(8,128)(2,1)}), bf16[4,1024,256]{2,1,0:T(8,128)(2,1)S(1)}, u32[]{:S(2)}, u32[]{:S(2)}) async-start(bf16[4,1024,256]{2,1,0:T(8,128)(2,1)} %bitcast.76), calls=%async_computation.1 | async-start | bytes 4194304 | tf_op jit(solution)/shard_map/all_to_all | solution.py:155
